TPU v7x, 32 devices: a whole 2x2x4 slice. The times are simulated.
32 devices in a mesh: dp: 4 (over z), fsdp: 2 (over x), rows: 4 (over y, core).
Axes of the slice: x: 2, y: 2, z: 4, core: 2. Of those that a mesh axis runs over, the one named last changes fastest.
Arguments:
- feature_maps: bfloat16 [8, 16, 32, 1536], P(('dp', 'fsdp'), 'rows'), may hold values from -30 to 30
- dw_kernel: float32 [7, 7, 1536], replicated, may hold values from -0.875 to 0.875
- norm_gain: float32 [1536], replicated, may hold values from 0.5 to 1.5
- w_up: bfloat16 [1536, 6144], P(('dp', 'rows'), 'fsdp'), may hold values from -0.15625 to 0.15625
- w_down: bfloat16 [6144, 1536], P('fsdp', ('dp', 'rows')), may hold values from -0.078125 to 0.078125
- layer_scale: float32 [1536], replicated, may hold values from 0.3 to 1.5
- d_out: bfloat16 [8, 16, 32, 1536], P(('dp', 'fsdp'), 'rows'), may hold values from -20 to 20
Outputs:
- result: bfloat16 [8, 16, 32, 1536], P(('dp', 'fsdp'), 'rows')
- grad_x: bfloat16 [8, 16, 32, 1536], P(('dp', 'fsdp'), 'rows')
- grad_up: float32 [1536, 6144], P(('dp', 'rows'), 'fsdp')
- grad_down: float32 [6144, 1536], P('fsdp', ('dp', 'rows'))
- grad_kernel: float32 [7, 7, 1536], replicated
- grad_gain: float32 [1536], replicated
- grad_scale: float32 [1536], replicated
All inputs are finite; a program needn't handle non-finite values.
Results may differ from a plain program's by a relative error of at most 0.0075.
Values may be sent and summed in bfloat16 or wider, within the bound.
No kernel may reach another device: no remote copies, remote signals or barrier semaphores. Data moves between devices by JAX's collectives and lax.ppermute only.
A program may use at most 128 MiB of HBM per device.

v0:
```python
import math
import jax
import jax.numpy as jnp
from jax import lax
from jax.sharding import PartitionSpec as P

KS = 7
norm_eps = 1e-06
inv_root_two = 1.0 / math.sqrt(2.0)
inv_root_two_pi = 1.0 / math.sqrt(2.0 * math.pi)
contract_rows = (((0,), (0,)), ((), ()))
contract_cols = (((1,), (1,)), ((), ()))


def padded_2(x, sides, width):
    for axis, dim in sides:
        devices, length = (lax.axis_size(axis), x.shape[dim])
        up = [(i, (i + 1) % devices) for i in range(devices - 1)]
        down = [(j, i) for i, j in up]
        last = lax.slice_in_dim(x, length - width, length, axis=dim)
        leading = lax.slice_in_dim(x, 0, width, axis=dim)
        before = lax.ppermute(last, axis, up)
        after = lax.ppermute(leading, axis, down)
        x = jnp.concatenate([before, x, after], axis=dim)
    return x


def gelu_exact(values):
    return 0.5 * values * (1.0 + jax.scipy.special.erf(values * inv_root_two))


def gelu_slope(values):
    cdf_part = 0.5 * (1.0 + jax.scipy.special.erf(values * inv_root_two))
    return cdf_part + values * jnp.exp(-0.5 * values * values) * inv_root_two_pi


def small_sums(kernel_part, gain_part, scale_part, width):
    every = ("dp", "fsdp", "rows")
    devices = lax.axis_size(every)
    packed = jnp.concatenate(
        [kernel_part.reshape(KS * KS, width), gain_part[None], scale_part[None]], axis=0
    )
    count = packed.shape[0]
    per = -(-count // devices)
    packed = jnp.pad(packed, ((0, per * devices - count), (0, 0)))
    mine = lax.all_to_all(packed.reshape(devices, per, width), every, 0, 0, tiled=True).sum(0)
    spread = jnp.broadcast_to(mine[None], (devices, per, width))
    total = lax.all_to_all(spread, every, 0, 0, tiled=True).reshape(devices * per, width)
    kernel_sum = total[: KS * KS].reshape(KS, KS, width)
    return (kernel_sum, total[KS * KS], total[KS * KS + 1])


def body(feature_maps, dw_kernel, norm_gain, w_up, w_down, layer_scale, d_out):
    scenes, strip, across, width = feature_maps.shape
    cells = scenes * strip * across
    hid_axes = ("fsdp", "rows")
    dp_size, row_size = (lax.axis_size("dp"), lax.axis_size("rows"))
    block_c, hid_f = w_up.shape
    sub = hid_f // row_size
    pieces = w_up.reshape(block_c, row_size, sub).transpose(1, 0, 2)
    pieces = jnp.broadcast_to(pieces[None], (dp_size, row_size, block_c, sub))
    pieces = pieces.reshape(dp_size * row_size, block_c, sub)
    up_loc = lax.all_to_all(pieces, ("dp", "rows"), 0, 0, tiled=True)
    up_loc = up_loc.reshape(dp_size * row_size * block_c, sub)
    down_loc = lax.all_to_all(w_down, "rows", 0, 1, tiled=True)
    down_loc = lax.all_gather(down_loc, "dp", axis=1, tiled=True)
    cotan = d_out.reshape(cells, width).astype(jnp.float32)
    back = (cotan * layer_scale).astype(jnp.bfloat16)
    rimmed = padded_2(feature_maps, (("rows", 1),), 3)
    padded = jnp.pad(rimmed.astype(jnp.float32), ((0, 0), (0, 0), (3, 3), (0, 0)))
    filtered = jnp.zeros(feature_maps.shape, jnp.float32)
    for row_off in range(KS):
        for col_off in range(KS):
            filtered = (
                filtered
                + padded[:, row_off : row_off + strip, col_off : col_off + across, :]
                * dw_kernel[row_off, col_off]
            )
    flat = filtered.reshape(cells, width)
    average = jnp.mean(flat, axis=-1, keepdims=True)
    center = flat - average
    variance = jnp.mean(center * center, axis=-1, keepdims=True)
    rstd = lax.rsqrt(variance + norm_eps)
    normed = center * rstd
    scaled = (normed * norm_gain).astype(jnp.bfloat16)
    pair = lax.all_gather(jnp.stack([scaled, back]), hid_axes, axis=1, tiled=True)
    gathered, back_all = (pair[0], pair[1])
    hidden = jnp.dot(gathered, up_loc, preferred_element_type=jnp.float32)
    active = gelu_exact(hidden).astype(jnp.bfloat16)
    mlp_terms = jnp.dot(active, down_loc, preferred_element_type=jnp.float32)
    down_part_t = lax.dot_general(
        back_all, active, contract_rows, preferred_element_type=jnp.float32
    )
    slope_in = lax.dot_general(
        back_all, down_loc, contract_cols, preferred_element_type=jnp.float32
    )
    hidden_grad = (slope_in * gelu_slope(hidden)).astype(jnp.bfloat16)
    up_part = lax.dot_general(
        gathered, hidden_grad, contract_rows, preferred_element_type=jnp.float32
    )
    norm_terms = lax.dot_general(
        hidden_grad, up_loc, contract_cols, preferred_element_type=jnp.float32
    )
    sums = lax.psum_scatter(
        jnp.stack([mlp_terms, norm_terms]).astype(jnp.bfloat16),
        hid_axes,
        scatter_dimension=1,
        tiled=True,
    ).astype(jnp.float32)
    branch, norm_grad = (sums[0], sums[1])
    resid = feature_maps.reshape(cells, width).astype(jnp.float32)
    result = (resid + layer_scale * branch).astype(jnp.bfloat16).reshape(feature_maps.shape)
    scale_part = jnp.sum(cotan * branch, axis=0)
    down_blocks = down_part_t.astype(jnp.bfloat16).reshape(dp_size, -1, sub)
    down_sum = lax.all_to_all(down_blocks, "dp", 0, 0, tiled=True).astype(jnp.float32).sum(0)
    up_sum = lax.psum_scatter(up_part.astype(jnp.bfloat16), "dp", scatter_dimension=0, tiled=True)
    grad_sums = jnp.stack([up_sum, down_sum.astype(jnp.bfloat16)])
    gain_part = jnp.sum(norm_grad * normed, axis=0)
    scaled_grad = norm_grad * norm_gain
    conv_grad = rstd * (
        scaled_grad
        - jnp.mean(scaled_grad, axis=-1, keepdims=True)
        - normed * jnp.mean(scaled_grad * normed, axis=-1, keepdims=True)
    )
    conv_grad = conv_grad.reshape(feature_maps.shape)
    grad_rim = padded_2(conv_grad.astype(jnp.bfloat16), (("rows", 1),), 3).astype(conv_grad.dtype)
    grad_pad = jnp.pad(grad_rim, ((0, 0), (0, 0), (3, 3), (0, 0)))
    kernel_rows = []
    back_conv = jnp.zeros(feature_maps.shape, jnp.float32)
    for row_off in range(KS):
        for col_off in range(KS):
            window = padded[:, row_off : row_off + strip, col_off : col_off + across, :]
            kernel_rows.append(jnp.sum(window * conv_grad, axis=(0, 1, 2)))
            back_conv = (
                back_conv
                + grad_pad[
                    :, 6 - row_off : 6 - row_off + strip, 6 - col_off : 6 - col_off + across, :
                ]
                * dw_kernel[row_off, col_off]
            )
    kernel_part = jnp.stack(kernel_rows).reshape(KS, KS, width)
    grad_x = (d_out.astype(jnp.float32) + back_conv).astype(jnp.bfloat16)
    grad_kernel, grad_gain, grad_scale = small_sums(kernel_part, gain_part, scale_part, width)
    grad_sums, grad_x, grad_kernel, grad_gain, grad_scale = lax.optimization_barrier(
        (grad_sums, grad_x, grad_kernel, grad_gain, grad_scale)
    )
    grad_sums = lax.all_to_all(grad_sums, "rows", 1, 2, tiled=True).astype(jnp.float32)
    grad_up, grad_down = (grad_sums[0], grad_sums[1].T)
    return (result, grad_x, grad_up, grad_down, grad_kernel, grad_gain, grad_scale)


def solution(mesh):
    return jax.shard_map(
        body,
        mesh=mesh,
        in_specs=(
            P(("dp", "fsdp"), "rows", None, None),
            P(),
            P(),
            P(("dp", "rows"), "fsdp"),
            P("fsdp", ("dp", "rows")),
            P(),
            P(("dp", "fsdp"), "rows", None, None),
        ),
        out_specs=(
            P(("dp", "fsdp"), "rows", None, None),
            P(("dp", "fsdp"), "rows", None, None),
            P(("dp", "rows"), "fsdp"),
            P("fsdp", ("dp", "rows")),
            P(),
            P(),
            P(),
        ),
        check_vma=False,
    )
```

profile of v0, /device:TPU:0, one launch (start us, length us, event | category | flops | bytes accessed | tf_op | source)
XLA Modules:
  0.0 350.1 jit_solution(6042365886521894993)
XLA Ops:
  7.2 1.1 fusion.114
  8.3 2.4 collective-permute-start
  10.7 1.3 collective-permute-start.1
  12.0 1.4 slice_reduce_fusion.48
  13.5 1.8 slice_reduce_fusion.50
  15.4 2.5 slice_reduce_fusion.49
  18.0 1.1 maximum_convert_fusion
  19.2 9.4 %fusion.110 = (f32[4,32]{1,0:T(4,128)S(1)}, f32[1,4,32,1536]{3,2,1,0:T(8,128)S(1)}) fusion(f32[1536]{0:T(1024)S(1)} %get-tuple-element.119, f32[1536]{0:T(1024)S(1)} %get-tuple-element.120, f32[1536]{0:T(1024)S(1)} %get-tuple-element.73, f32[1536]{0:T(1024)S(1)} %get-tuple-element.74, f32[1,10,32,1536]{3,2,1,0:T(8,128)S(1)} %maximum_convert_fusion, ...), kind=kLoop, calls=%fused_computation.332 | loop fusion | flops 19267456 | bytes 8641024 | tf_op jit(solution)/shard_map/reduce_sum | solution.py:80
  29.8 0.9 pad_maximum_fusion.2
  31.0 0.9 copy.45
  31.9 6.1 %all-to-all-start.1 = ((bf16[4,768,96]{1,2,0:T(8,128)(2,1)}), bf16[4,768,96]{1,2,0:T(8,128)(2,1)S(1)}, u32[]{:S(2)}, u32[]{:S(2)}) async-start(bf16[4,768,96]{1,2,0:T(8,128)(2,1)} %bitcast.94), calls=%async_computation.1 | async-start | bytes 1179648 | tf_op jit(solution)/shard_map/all_to_all | solution.py:65
  38.0 2.5 reshape.558
  40.5 2.0 copy.34
  42.5 7.0 %all-to-all-done.1 = bf16[4,768,96]{1,2,0:T(8,128)(2,1)S(1)} async-done(((bf16[4,768,96]{1,2,0:T(8,128)(2,1)}), bf16[4,768,96]{1,2,0:T(8,128)(2,1)S(1)}, u32[]{:S(2)}, u32[]{:S(2)}) %all-to-all-start.1) | async-done | bytes 589856 | tf_op jit(solution)/shard_map/all_to_all | solution.py:65
  49.5 2.9 broadcast_in_dim.8
  52.4 5.3 %all-to-all-start = ((bf16[16,96,768]{2,1,0:T(8,128)(2,1)}), bf16[16,96,768]{2,1,0:T(8,128)(2,1)}, u32[]{:S(2)}, u32[]{:S(2)}) async-start(bf16[16,96,768]{2,1,0:T(8,128)(2,1)} %bitcast.86), calls=%async_computation | async-start | bytes 4718592 | tf_op jit(solution)/shard_map/all_to_all | solution.py:63
  57.8 0.7 all-gather.5.cloned.1.call-update
  58.8 44.8 %all-to-all-done = bf16[16,96,768]{2,1,0:T(8,128)(2,1)} async-done(((bf16[16,96,768]{2,1,0:T(8,128)(2,1)}), bf16[16,96,768]{2,1,0:T(8,128)(2,1)}, u32[]{:S(2)}, u32[]{:S(2)}) %all-to-all-start) | async-done | bytes 2359328 | tf_op jit(solution)/shard_map/all_to_all | solution.py:63
  103.6 7.5 %multiply_convert_fusion = (bf16[1024,768]{1,0:T(8,128)(2,1)}, f32[1024,768]{1,0:T(8,128)}) fusion(bf16[1536,768]{1,0:T(8,128)(2,1)} %bitcast.5, bf16[2,1024,1536]{2,1,0:T(8,128)(2,1)} %all-gather.3.cloned.1.call-done), kind=kOutput, calls=%fused_computation.100 | convolution fusion | flops 2419851264 | bytes 10223616 | tf_op jit(solution)/shard_map/dot_general | solution.py:88
  111.1 43.2 %all-gather.5.cloned.1.call-done = bf16[768,1536]{0,1:T(8,128)(2,1)} async-done(((bf16[768,384]{0,1:T(8,128)(2,1)}), bf16[768,1536]{0,1:T(8,128)(2,1)}) %all-gather.5.cloned.1.call-update) | async-done | bytes 2359312 | tf_op jit(solution)/shard_map/all_gather | solution.py:66
  154.3 6.6 %fusion.7 = bf16[1024,768]{1,0:T(8,128)(2,1)S(1)} fusion(f32[1024,768]{1,0:T(8,128)} %get-tuple-element.134, bf16[768,1536]{0,1:T(8,128)(2,1)} %all-gather.5.cloned.1.call-done, bf16[2,1024,1536]{2,1,0:T(8,128)(2,1)} %all-gather.3.cloned.1.call-done), kind=kOutput, calls=%fused_computation.97 | convolution fusion | flops 2423783424 | bytes 10223616 | tf_op jit(solution)/shard_map/dot_general | solution.py:94
  161.0 5.1 %fusion.1 = bf16[1,1024,1536]{2,1,0:T(8,128)(2,1)S(1)} fusion(bf16[1024,768]{1,0:T(8,128)(2,1)S(1)} %fusion.7, bf16[1536,768]{1,0:T(8,128)(2,1)} %bitcast.5), kind=kOutput, calls=%fused_computation.91 | convolution fusion | flops 2417491968 | bytes 7077888 | tf_op jit(solution)/shard_map/dot_general | solution.py:101
  166.1 2.9 fusion
  169.1 3.2 pad_maximum_fusion
  172.8 6.5 %convolution_convert_fusion.3 = bf16[1536,768]{1,0:T(8,128)(2,1)} fusion(bf16[1024,768]{1,0:T(8,128)(2,1)} %copy-done.61, bf16[2,1024,1536]{2,1,0:T(8,128)(2,1)} %all-gather.3.cloned.1.call-done), kind=kOutput, calls=%fused_computation.89 | convolution fusion | flops 2417098752 | bytes 7077888 | tf_op jit(solution)/shard_map/dot_general | solution.py:98
  179.3 7.1 %convolution_convert_fusion.2 = bf16[1536,768]{1,0:T(8,128)(2,1)} fusion(bf16[1024,768]{1,0:T(8,128)(2,1)} %get-tuple-element.133, bf16[2,1024,1536]{2,1,0:T(8,128)(2,1)} %all-gather.3.cloned.1.call-done), kind=kOutput, calls=%fused_computation.88 | convolution fusion | flops 2417098752 | bytes 7077888 | tf_op jit(solution)/shard_map/dot_general | solution.py:91
  186.4 4.5 %all-to-all-start.2 = ((bf16[4,384,768]{2,1,0:T(8,128)(2,1)}), bf16[4,384,768]{2,1,0:T(8,128)(2,1)}, u32[]{:S(2)}, u32[]{:S(2)}) async-start(bf16[4,384,768]{2,1,0:T(8,128)(2,1)} %bitcast.92), calls=%async_computation.4 | async-start | bytes 4718592 | tf_op jit(solution)/shard_map/all_to_all | solution.py:115
  190.9 42.1 %reduce-scatter.3.cloned.1.call-done = bf16[2,128,1536]{2,1,0:T(8,128)(2,1)} async-done(((bf16[2,1024,1536]{2,1,0:T(8,128)(2,1)}), bf16[2,128,1536]{2,1,0:T(8,128)(2,1)}) %reduce-scatter.3.cloned.1.call-update) | async-done | bytes 786448 | tf_op jit(solution)/shard_map/reduce_scatter | solution.py:104
  233.0 1.4 convert_element_type.120
  234.4 2.1 fusion.104
  237.6 1.3 div.22
  238.9 1.2 broadcast_multiply_fusion.1
  240.1 1.3 div.24
  241.4 1.3 broadcast_in_dim.10
  242.7 1.0 fusion.112
  243.7 2.4 multiply_reduce_fusion
  246.3 2.0 multiply_reduce_fusion.18
  248.4 1.4 multiply_reduce_fusion.36
  250.8 1.0 reshape.563
  251.8 4.7 %all-to-all-start.3 = ((f32[32,2,1536]{2,1,0:T(2,128)}), f32[32,2,1536]{2,1,0:T(2,128)}, u32[]{:S(2)}, u32[]{:S(2)}) async-start(f32[32,2,1536]{2,1,0:T(2,128)} %reshape.563), calls=%async_computation.5 | async-start | bytes 786432 | tf_op jit(solution)/shard_map/all_to_all | solution.py:46
  256.6 2.1 collective-permute-start.2
  258.7 1.5 collective-permute-start.3
  260.2 2.3 reduce_sum.518
  262.5 27.8 %reduce-scatter.5.cloned.1.call-done = bf16[384,768]{1,0:T(8,128)(2,1)} async-done(((bf16[1536,768]{1,0:T(8,128)(2,1)}), bf16[384,768]{1,0:T(8,128)(2,1)}) %reduce-scatter.5.cloned.1.call-update) | async-done | bytes 589840 | tf_op jit(solution)/shard_map/reduce_scatter | solution.py:116
  290.2 1.2 pad_maximum_fusion.1
  291.5 0.7 copy-done.5
  292.2 1.2 maximum_convert_fusion.1
  293.4 1.1 reduce_sum.572
  294.5 0.8 broadcast_in_dim.11
  295.3 4.9 %all-to-all-start.4 = ((f32[32,2,1536]{2,1,0:T(2,128)}), f32[32,2,1536]{2,1,0:T(2,128)S(1)}, u32[]{:S(2)}, u32[]{:S(2)}) async-start(f32[32,2,1536]{2,1,0:T(2,128)} %broadcast_in_dim.11), calls=%async_computation.6 | async-start | bytes 786432 | tf_op jit(solution)/shard_map/all_to_all | solution.py:48
  300.3 8.3 %fusion.97 = bf16[1,4,32,1536]{3,2,1,0:T(8,128)(2,1)} fusion(f32[1,10,32,1536]{3,2,1,0:T(8,128)S(1)} %maximum_convert_fusion.1, f32[1536]{0:T(1024)} %copy-done.16, f32[1536]{0:T(1024)} %copy-done.17, f32[1536]{0:T(1024)} %copy-done.19, f32[1536]{0:T(1024)} %copy-done.20, f32[1536]{0:T(1024)} %copy-done.21, f32[1536]{0:T(1024)} %copy-done.22, ...), kind=kLoop, calls=%fused_computation.195 | loop fusion | flops 19660800 | bytes 8562688 | tf_op jit(solution)/shard_map/convert_element_type | solution.py:142
  308.6 4.8 %all-to-all-done.4 = f32[32,2,1536]{2,1,0:T(2,128)S(1)} async-done(((f32[32,2,1536]{2,1,0:T(2,128)}), f32[32,2,1536]{2,1,0:T(2,128)S(1)}, u32[]{:S(2)}, u32[]{:S(2)}) %all-to-all-start.4) | async-done | bytes 393248 | tf_op jit(solution)/shard_map/all_to_all | solution.py:48
  313.8 0.6 slice_reduce_fusion
  314.4 0.8 reshape.565
  315.2 2.2 copy.37
  317.4 3.5 %all-to-all-start.5 = ((bf16[2,384,768]{2,0,1:T(2,128)(2,1)}), bf16[2,384,768]{2,0,1:T(2,128)(2,1)S(1)}, u32[]{:S(2)}, u32[]{:S(2)}) async-start(bf16[2,384,768]{2,0,1:T(2,128)(2,1)} %copy.37), calls=%async_computation.7 | async-start | bytes 2359296 | tf_op jit(solution)/shard_map/all_to_all | solution.py:147
  321.0 2.0 add_convert_fusion
  322.9 13.8 %all-to-all-done.5 = bf16[2,384,768]{2,0,1:T(2,128)(2,1)S(1)} async-done(((bf16[2,384,768]{2,0,1:T(2,128)(2,1)}), bf16[2,384,768]{2,0,1:T(2,128)(2,1)S(1)}, u32[]{:S(2)}, u32[]{:S(2)}) %all-to-all-start.5) | async-done | bytes 1179680 | tf_op jit(solution)/shard_map/all_to_all | solution.py:147
  336.8 0.8 convert_bitcast_fusion
  337.6 1.8 fusion.111
  339.4 0.8 copy.39
  340.2 1.2 copy.43
  341.4 0.8 copy.38
  342.2 1.2 copy.42
  (199 shorter events, 4.4 us)
Async XLA Ops:
  7.2 96.4 %all-gather.3.cloned.1.call-start = ((), (), s32[]{:S(2)}) async-start(), calls=%async_computation.8 | async-start | bytes 7077888 | tf_op jit(solution)/shard_map/all_gather | solution.py:86
  8.3 9.7 %collective-permute-start = (bf16[1,3,32,1536]{3,2,1,0:T(8,128)(2,1)S(1)}, bf16[1,3,32,1536]{3,2,1,0:T(8,128)(2,1)S(1)}, u32[]{:S(2)}, u32[]{:S(2)}) collective-permute-start(bf16[1,3,32,1536]{3,2,1,0:T(8,128)(2,1)S(1)} %get-tuple-element.131), channel_id=1, source_target_pairs={{0,1},{1,2},{2,3},{4,5},{5,6},{6,7},{8,9},{9,10},{10,11},{12,13},{... | collective-permute-start | bytes 884744 | tf_op jit(solution)/shard_map/ppermute | solution.py:22
  10.7 7.3 %collective-permute-start.1 = (bf16[1,3,32,1536]{3,2,1,0:T(8,128)(2,1)S(1)}, bf16[1,3,32,1536]{3,2,1,0:T(8,128)(2,1)S(1)}, u32[]{:S(2)}, u32[]{:S(2)}) collective-permute-start(bf16[1,3,32,1536]{3,2,1,0:T(8,128)(2,1)S(1)} %get-tuple-element.132), channel_id=1, source_target_pairs={{1,0},{2,1},{3,2},{5,4},{6,5},{7,6},{9,8},{10,9},{11,10},{13,12},{... | collective-permute-start | bytes 884744 | tf_op jit(solution)/shard_map/ppermute | solution.py:23
  13.4 15.3 %copy-start.7 = (f32[1536]{0:T(1024)}, f32[1536]{0:T(1024)S(1)}, u32[]{:S(2)}) copy-start(f32[1536]{0:T(1024)S(1)} %get-tuple-element.111) | copy-start | bytes 18436
  13.4 15.3 %copy-start.9 = (f32[1536]{0:T(1024)}, f32[1536]{0:T(1024)S(1)}, u32[]{:S(2)}) copy-start(f32[1536]{0:T(1024)S(1)} %get-tuple-element.112) | copy-start | bytes 18436
  13.4 15.3 %copy-start.10 = (f32[1536]{0:T(1024)}, f32[1536]{0:T(1024)S(1)}, u32[]{:S(2)}) copy-start(f32[1536]{0:T(1024)S(1)} %get-tuple-element.113) | copy-start | bytes 18436
  13.4 15.3 %copy-start.11 = (f32[1536]{0:T(1024)}, f32[1536]{0:T(1024)S(1)}, u32[]{:S(2)}) copy-start(f32[1536]{0:T(1024)S(1)} %get-tuple-element.114) | copy-start | bytes 18436
  13.4 15.3 %copy-start.12 = (f32[1536]{0:T(1024)}, f32[1536]{0:T(1024)S(1)}, u32[]{:S(2)}) copy-start(f32[1536]{0:T(1024)S(1)} %get-tuple-element.115) | copy-start | bytes 18436
  13.4 15.3 %copy-start.13 = (f32[1536]{0:T(1024)}, f32[1536]{0:T(1024)S(1)}, u32[]{:S(2)}) copy-start(f32[1536]{0:T(1024)S(1)} %get-tuple-element.116) | copy-start | bytes 18436
  13.4 15.3 %copy-start.14 = (f32[1536]{0:T(1024)}, f32[1536]{0:T(1024)S(1)}, u32[]{:S(2)}) copy-start(f32[1536]{0:T(1024)S(1)} %get-tuple-element.117) | copy-start | bytes 18436
  13.4 15.3 %copy-start.15 = (f32[1536]{0:T(1024)}, f32[1536]{0:T(1024)S(1)}, u32[]{:S(2)}) copy-start(f32[1536]{0:T(1024)S(1)} %get-tuple-element.118) | copy-start | bytes 18436
  13.5 15.3 %copy-start.16 = (f32[1536]{0:T(1024)}, f32[1536]{0:T(1024)S(1)}, u32[]{:S(2)}) copy-start(f32[1536]{0:T(1024)S(1)} %get-tuple-element.119) | copy-start | bytes 18436
  13.5 15.3 %copy-start.17 = (f32[1536]{0:T(1024)}, f32[1536]{0:T(1024)S(1)}, u32[]{:S(2)}) copy-start(f32[1536]{0:T(1024)S(1)} %get-tuple-element.120) | copy-start | bytes 18436
  15.2 13.5 %copy-start.18 = (f32[1536]{0:T(1024)}, f32[1536]{0:T(1024)S(1)}, u32[]{:S(2)}) copy-start(f32[1536]{0:T(1024)S(1)} %get-tuple-element.72) | copy-start | bytes 18436
  15.3 13.5 %copy-start.19 = (f32[1536]{0:T(1024)}, f32[1536]{0:T(1024)S(1)}, u32[]{:S(2)}) copy-start(f32[1536]{0:T(1024)S(1)} %get-tuple-element.73) | copy-start | bytes 18436
  15.3 13.5 %copy-start.20 = (f32[1536]{0:T(1024)}, f32[1536]{0:T(1024)S(1)}, u32[]{:S(2)}) copy-start(f32[1536]{0:T(1024)S(1)} %get-tuple-element.74) | copy-start | bytes 18436
  15.3 13.5 %copy-start.21 = (f32[1536]{0:T(1024)}, f32[1536]{0:T(1024)S(1)}, u32[]{:S(2)}) copy-start(f32[1536]{0:T(1024)S(1)} %get-tuple-element.75) | copy-start | bytes 18436
  15.3 13.5 %copy-start.22 = (f32[1536]{0:T(1024)}, f32[1536]{0:T(1024)S(1)}, u32[]{:S(2)}) copy-start(f32[1536]{0:T(1024)S(1)} %get-tuple-element.76) | copy-start | bytes 18436
  15.3 13.5 %copy-start.23 = (f32[1536]{0:T(1024)}, f32[1536]{0:T(1024)S(1)}, u32[]{:S(2)}) copy-start(f32[1536]{0:T(1024)S(1)} %get-tuple-element.77) | copy-start | bytes 18436
  15.3 13.5 %copy-start.24 = (f32[1536]{0:T(1024)}, f32[1536]{0:T(1024)S(1)}, u32[]{:S(2)}) copy-start(f32[1536]{0:T(1024)S(1)} %get-tuple-element.78) | copy-start | bytes 18436
  15.3 13.5 %copy-start.25 = (f32[1536]{0:T(1024)}, f32[1536]{0:T(1024)S(1)}, u32[]{:S(2)}) copy-start(f32[1536]{0:T(1024)S(1)} %get-tuple-element.79) | copy-start | bytes 18436
  15.3 13.5 %copy-start.26 = (f32[1536]{0:T(1024)}, f32[1536]{0:T(1024)S(1)}, u32[]{:S(2)}) copy-start(f32[1536]{0:T(1024)S(1)} %get-tuple-element.80) | copy-start | bytes 18436
  15.3 13.5 %copy-start.27 = (f32[1536]{0:T(1024)}, f32[1536]{0:T(1024)S(1)}, u32[]{:S(2)}) copy-start(f32[1536]{0:T(1024)S(1)} %get-tuple-element.81) | copy-start | bytes 18436
  15.3 13.5 %copy-start.28 = (f32[1536]{0:T(1024)}, f32[1536]{0:T(1024)S(1)}, u32[]{:S(2)}) copy-start(f32[1536]{0:T(1024)S(1)} %get-tuple-element.82) | copy-start | bytes 18436
  15.4 13.5 %copy-start.29 = (f32[1536]{0:T(1024)}, f32[1536]{0:T(1024)S(1)}, u32[]{:S(2)}) copy-start(f32[1536]{0:T(1024)S(1)} %get-tuple-element.83) | copy-start | bytes 18436
  15.4 13.5 %copy-start.30 = (f32[1536]{0:T(1024)}, f32[1536]{0:T(1024)S(1)}, u32[]{:S(2)}) copy-start(f32[1536]{0:T(1024)S(1)} %get-tuple-element.84) | copy-start | bytes 18436
  15.4 13.5 %copy-start.31 = (f32[1536]{0:T(1024)}, f32[1536]{0:T(1024)S(1)}, u32[]{:S(2)}) copy-start(f32[1536]{0:T(1024)S(1)} %get-tuple-element.85) | copy-start | bytes 18436
  15.4 13.5 %copy-start.32 = (f32[1536]{0:T(1024)}, f32[1536]{0:T(1024)S(1)}, u32[]{:S(2)}) copy-start(f32[1536]{0:T(1024)S(1)} %get-tuple-element.86) | copy-start | bytes 18436
  15.4 13.5 %copy-start.33 = (f32[1536]{0:T(1024)}, f32[1536]{0:T(1024)S(1)}, u32[]{:S(2)}) copy-start(f32[1536]{0:T(1024)S(1)} %get-tuple-element.87) | copy-start | bytes 18436
  15.4 13.5 %copy-start.34 = (f32[1536]{0:T(1024)}, f32[1536]{0:T(1024)S(1)}, u32[]{:S(2)}) copy-start(f32[1536]{0:T(1024)S(1)} %get-tuple-element.88) | copy-start | bytes 18436
  15.4 13.5 %copy-start.35 = (f32[1536]{0:T(1024)}, f32[1536]{0:T(1024)S(1)}, u32[]{:S(2)}) copy-start(f32[1536]{0:T(1024)S(1)} %get-tuple-element.89) | copy-start | bytes 18436
  15.4 13.5 %copy-start.36 = (f32[1536]{0:T(1024)}, f32[1536]{0:T(1024)S(1)}, u32[]{:S(2)}) copy-start(f32[1536]{0:T(1024)S(1)} %get-tuple-element.90) | copy-start | bytes 18436
  17.9 11.0 %copy-start.37 = (f32[1536]{0:T(1024)}, f32[1536]{0:T(1024)S(1)}, u32[]{:S(2)}) copy-start(f32[1536]{0:T(1024)S(1)} %get-tuple-element.91) | copy-start | bytes 18436
  17.9 11.0 %copy-start.38 = (f32[1536]{0:T(1024)}, f32[1536]{0:T(1024)S(1)}, u32[]{:S(2)}) copy-start(f32[1536]{0:T(1024)S(1)} %get-tuple-element.92) | copy-start | bytes 18436
  17.9 11.0 %copy-start.39 = (f32[1536]{0:T(1024)}, f32[1536]{0:T(1024)S(1)}, u32[]{:S(2)}) copy-start(f32[1536]{0:T(1024)S(1)} %get-tuple-element.93) | copy-start | bytes 18436
  17.9 11.0 %copy-start.40 = (f32[1536]{0:T(1024)}, f32[1536]{0:T(1024)S(1)}, u32[]{:S(2)}) copy-start(f32[1536]{0:T(1024)S(1)} %get-tuple-element.94) | copy-start | bytes 18436
  18.0 11.0 %copy-start.41 = (f32[1536]{0:T(1024)}, f32[1536]{0:T(1024)S(1)}, u32[]{:S(2)}) copy-start(f32[1536]{0:T(1024)S(1)} %get-tuple-element.95) | copy-start | bytes 18436
  18.0 11.0 %copy-start.42 = (f32[1536]{0:T(1024)}, f32[1536]{0:T(1024)S(1)}, u32[]{:S(2)}) copy-start(f32[1536]{0:T(1024)S(1)} %get-tuple-element.96) | copy-start | bytes 18436
  18.0 11.0 %copy-start.43 = (f32[1536]{0:T(1024)}, f32[1536]{0:T(1024)S(1)}, u32[]{:S(2)}) copy-start(f32[1536]{0:T(1024)S(1)} %get-tuple-element.97) | copy-start | bytes 18436
  18.0 11.0 %copy-start.44 = (f32[1536]{0:T(1024)}, f32[1536]{0:T(1024)S(1)}, u32[]{:S(2)}) copy-start(f32[1536]{0:T(1024)S(1)} %get-tuple-element.98) | copy-start | bytes 18436
  18.0 11.0 %copy-start.45 = (f32[1536]{0:T(1024)}, f32[1536]{0:T(1024)S(1)}, u32[]{:S(2)}) copy-start(f32[1536]{0:T(1024)S(1)} %get-tuple-element.99) | copy-start | bytes 18436
  18.0 11.0 %copy-start.46 = (f32[1536]{0:T(1024)}, f32[1536]{0:T(1024)S(1)}, u32[]{:S(2)}) copy-start(f32[1536]{0:T(1024)S(1)} %get-tuple-element.100) | copy-start | bytes 18436
  19.2 10.3 %copy-start.2 = (bf16[1,4,32,1536]{3,2,1,0:T(8,128)(2,1)S(1)}, bf16[1,4,32,1536]{3,2,1,0:T(8,128)(2,1)}, u32[]{:S(2)}) copy-start(bf16[1,4,32,1536]{3,2,1,0:T(8,128)(2,1)} %param.13) | copy-start | bytes 1179652
  19.2 10.3 %copy-start.6 = (f32[1536]{0:T(1024)S(1)}, f32[1536]{0:T(1024)}, u32[]{:S(2)}) copy-start(f32[1536]{0:T(1024)} %param.9) | copy-start | bytes 18436
  19.2 10.3 %copy-start.47 = (f32[1536]{0:T(1024)S(1)}, f32[1536]{0:T(1024)}, u32[]{:S(2)}) copy-start(f32[1536]{0:T(1024)} %param.12) | copy-start | bytes 18436
  31.9 17.6 %all-to-all-start.1 = ((bf16[4,768,96]{1,2,0:T(8,128)(2,1)}), bf16[4,768,96]{1,2,0:T(8,128)(2,1)S(1)}, u32[]{:S(2)}, u32[]{:S(2)}) async-start(bf16[4,768,96]{1,2,0:T(8,128)(2,1)} %bitcast.94), calls=%async_computation.1 | async-start | bytes 1179648 | tf_op jit(solution)/shard_map/all_to_all | solution.py:65
  49.5 2.9 copy-start.3
  52.4 51.2 %all-to-all-start = ((bf16[16,96,768]{2,1,0:T(8,128)(2,1)}), bf16[16,96,768]{2,1,0:T(8,128)(2,1)}, u32[]{:S(2)}, u32[]{:S(2)}) async-start(bf16[16,96,768]{2,1,0:T(8,128)(2,1)} %bitcast.86), calls=%async_computation | async-start | bytes 4718592 | tf_op jit(solution)/shard_map/all_to_all | solution.py:63
  57.7 96.6 %all-gather.5.cloned.1.call-start = ((), (), s32[]{:S(2)}) async-start(), calls=%async_computation.9 | async-start | bytes 2949120 | tf_op jit(solution)/shard_map/all_gather | solution.py:66
  58.5 174.5 %reduce-scatter.3.cloned.1.call-start = ((), (), s32[]{:S(2)}) async-start(), calls=%async_computation.10 | async-start | bytes 7077888 | tf_op jit(solution)/shard_map/reduce_scatter | solution.py:104
  160.9 5.2 %copy-start.61 = (bf16[1024,768]{1,0:T(8,128)(2,1)}, bf16[1024,768]{1,0:T(8,128)(2,1)S(1)}, u32[]{:S(2)}) copy-start(bf16[1024,768]{1,0:T(8,128)(2,1)S(1)} %fusion.7) | copy-start | bytes 4718596
  161.0 5.2 %copy-start.59 = (bf16[768,1536]{0,1:T(8,128)(2,1)S(1)}, bf16[768,1536]{0,1:T(8,128)(2,1)}, u32[]{:S(2)}) copy-start(bf16[768,1536]{0,1:T(8,128)(2,1)} %all-gather.5.cloned.1.call-done) | copy-start | bytes 7077892
  161.0 5.2 %copy-start.60 = (bf16[1024,768]{1,0:T(8,128)(2,1)S(1)}, bf16[1024,768]{1,0:T(8,128)(2,1)}, u32[]{:S(2)}) copy-start(bf16[1024,768]{1,0:T(8,128)(2,1)} %get-tuple-element.133) | copy-start | bytes 4718596
  172.3 118.0 %reduce-scatter.5.cloned.1.call-start = ((), (), s32[]{:S(2)}) async-start(), calls=%async_computation.11 | async-start | bytes 2949120 | tf_op jit(solution)/shard_map/reduce_scatter | solution.py:116
  186.4 65.4 %all-to-all-start.2 = ((bf16[4,384,768]{2,1,0:T(8,128)(2,1)}), bf16[4,384,768]{2,1,0:T(8,128)(2,1)}, u32[]{:S(2)}, u32[]{:S(2)}) async-start(bf16[4,384,768]{2,1,0:T(8,128)(2,1)} %bitcast.92), calls=%async_computation.4 | async-start | bytes 4718592 | tf_op jit(solution)/shard_map/all_to_all | solution.py:115
  233.0 9.7 %copy-start = (bf16[2,128,1536]{2,1,0:T(8,128)(2,1)S(1)}, bf16[2,128,1536]{2,1,0:T(8,128)(2,1)}, u32[]{:S(2)}) copy-start(bf16[2,128,1536]{2,1,0:T(8,128)(2,1)} %reduce-scatter.3.cloned.1.call-done) | copy-start | bytes 2359300
  251.8 41.5 %all-to-all-start.3 = ((f32[32,2,1536]{2,1,0:T(2,128)}), f32[32,2,1536]{2,1,0:T(2,128)}, u32[]{:S(2)}, u32[]{:S(2)}) async-start(f32[32,2,1536]{2,1,0:T(2,128)} %reshape.563), calls=%async_computation.5 | async-start | bytes 786432 | tf_op jit(solution)/shard_map/all_to_all | solution.py:46
  256.6 34.9 %collective-permute-start.2 = (bf16[1,3,32,1536]{3,2,1,0:T(8,128)(2,1)S(1)}, bf16[1,3,32,1536]{3,2,1,0:T(8,128)(2,1)S(1)}, u32[]{:S(2)}, u32[]{:S(2)}) collective-permute-start(bf16[1,3,32,1536]{3,2,1,0:T(8,128)(2,1)S(1)} %get-tuple-element.129), channel_id=1, source_target_pairs={{0,1},{1,2},{2,3},{4,5},{5,6},{6,7},{8,9},{9,10},{10,11},{12,13},{... | collective-permute-start | bytes 884744 | tf_op jit(solution)/shard_map/ppermute | solution.py:22
  258.7 33.5 %collective-permute-start.3 = (bf16[1,3,32,1536]{3,2,1,0:T(8,128)(2,1)S(1)}, bf16[1,3,32,1536]{3,2,1,0:T(8,128)(2,1)}, u32[]{:S(2)}, u32[]{:S(2)}) collective-permute-start(bf16[1,3,32,1536]{3,2,1,0:T(8,128)(2,1)S(1)} %get-tuple-element.130), channel_id=1, source_target_pairs={{1,0},{2,1},{3,2},{5,4},{6,5},{7,6},{9,8},{10,9},{11,10},{13,12},{... | collective-permute-start | bytes 884744 | tf_op jit(solution)/shard_map/ppermute | solution.py:23
  291.4 8.9 %copy-start.8 = (f32[1536]{0:T(1024)S(1)}, f32[1536]{0:T(1024)}, u32[]{:S(2)}) copy-start(f32[1536]{0:T(1024)} %copy-done.7) | copy-start | bytes 18436
  295.3 18.1 %all-to-all-start.4 = ((f32[32,2,1536]{2,1,0:T(2,128)}), f32[32,2,1536]{2,1,0:T(2,128)S(1)}, u32[]{:S(2)}, u32[]{:S(2)}) async-start(f32[32,2,1536]{2,1,0:T(2,128)} %broadcast_in_dim.11), calls=%async_computation.6 | async-start | bytes 786432 | tf_op jit(solution)/shard_map/all_to_all | solution.py:48
  315.2 5.8 %copy-start.1 = (bf16[1,4,32,1536]{3,2,1,0:T(8,128)(2,1)S(1)}, bf16[1,4,32,1536]{3,2,1,0:T(8,128)(2,1)}, u32[]{:S(2)}) copy-start(bf16[1,4,32,1536]{3,2,1,0:T(8,128)(2,1)} %param.7) | copy-start | bytes 1179652
  315.2 5.8 %copy-start.48 = (f32[1536]{0:T(1024)S(1)}, f32[1536]{0:T(1024)}, u32[]{:S(2)}) copy-start(f32[1536]{0:T(1024)} %param.12) | copy-start | bytes 18436
  317.4 19.4 %all-to-all-start.5 = ((bf16[2,384,768]{2,0,1:T(2,128)(2,1)}), bf16[2,384,768]{2,0,1:T(2,128)(2,1)S(1)}, u32[]{:S(2)}, u32[]{:S(2)}) async-start(bf16[2,384,768]{2,0,1:T(2,128)(2,1)} %copy.37), calls=%async_computation.7 | async-start | bytes 2359296 | tf_op jit(solution)/shard_map/all_to_all | solution.py:147
  (12 other events, 23.2 us)
Sparse Core Ops, SparseCore 0:
  30.9 67.5 all-gather.2
  100.6 53.6 all-gather.4
  172.4 60.5 reduce-scatter.2
  235.3 54.9 reduce-scatter.4
where the time goes:
time: 357 us; the launch traced here: 350 us
  waiting for transfers between devices  184 us (52%)
  other arithmetic  43 us (12%)
  starting transfers between devices  37.2 us (10%)
  matrix products  35.8 us (10%)
  local copies, waits for them, and re-layouts  34.4 us (10%)
  between operations  15.4 us (4%)
    all_to_all x1, waiting for transfers between devices, body(): up_loc = lax.all_to_all(pieces, ('dp', 'rows'), 0, 0, tiled=True)  44.8 us
    all_gather x1, waiting for transfers between devices, body(): down_loc = lax.all_gather(down_loc, 'dp', axis=1, tiled=True)  43.2 us
    reduce_scatter x1, waiting for transfers between devices, body(): lax.psum_scatter(jnp.stack([mlp_terms, norm_terms]).astype(jnp.bfloat16),...  42.1 us
    reduce_scatter x1, waiting for transfers between devices, body(): lax.psum_scatter(up_part.astype(jnp.bfloat16), 'dp', scatter_dimension=0,...  27.8 us
    all_to_all x1, waiting for transfers between devices, body(): lax.all_to_all(grad_sums, 'rows', 1, 2, tiled=True).astype(jnp.float32)  13.8 us
    reduce_sum x1, other arithmetic, body(): average = jnp.mean(flat, axis=-1, keepdims=True)  9.44 us
    convert_element_type x1, other arithmetic, body(): grad_x = (d_out.astype(jnp.float32) + back_conv).astype(jnp.bfloat16)  8.33 us
    dot_general x1, matrix products, body(): hidden = jnp.dot(gathered, up_loc, preferred_element_type=jnp.float32)  7.49 us
  transfers between devices with their start and end apart: 14, of which 7 were waited for; matrix products, arithmetic and copies ran while one was open for 20% of the time, Pallas kernels for 0%

commit v1 on v0

--- a/solution.py
+++ b/solution.py
@@ -10,6 +10,29 @@
 inv_root_two_pi = 1.0 / math.sqrt(2.0 * math.pi)
 contract_rows = (((0,), (0,)), ((), ()))
 contract_cols = (((1,), (1,)), ((), ()))
+
+
+def split_up(x, dim, count):
+    shape = x.shape
+    blocks = x.reshape(*shape[:dim], count, shape[dim] // count, *shape[dim + 1 :])
+    return jnp.moveaxis(blocks, dim, 0)
+
+
+def laid_out(parts, dim):
+    dims = list(parts.shape[1:])
+    dims[dim] *= parts.shape[0]
+    return jnp.moveaxis(parts, 0, dim).reshape(dims)
+
+
+def sent_to_each(x, axis, split_dim, concat_dim):
+    peers, index = (lax.axis_size(axis), lax.axis_index(axis))
+    tiles = split_up(x, split_dim, peers)
+    outs = [tiles[index]]
+    for step in range(1, peers):
+        sent = tiles[(index + step) % peers]
+        outs.append(lax.ppermute(sent, axis, [(i, (i + step) % peers) for i in range(peers)]))
+    tiles = jnp.stack(outs)[(index - jnp.arange(peers)) % peers]
+    return laid_out(tiles, concat_dim)
 
 
 def padded_2(x, sides, width):
@@ -144,7 +167,7 @@
     grad_sums, grad_x, grad_kernel, grad_gain, grad_scale = lax.optimization_barrier(
         (grad_sums, grad_x, grad_kernel, grad_gain, grad_scale)
     )
-    grad_sums = lax.all_to_all(grad_sums, "rows", 1, 2, tiled=True).astype(jnp.float32)
+    grad_sums = sent_to_each(grad_sums, "rows", 1, 2).astype(jnp.float32)
     grad_up, grad_down = (grad_sums[0], grad_sums[1].T)
     return (result, grad_x, grad_up, grad_down, grad_kernel, grad_gain, grad_scale)
 

time: 357 us -> 343 us (0.961); the launches traced: 350 us -> 342 us
    all_to_all x1 -> x0, waiting for transfers between devices: 13.8 us -> none  [body(): lax.all_to_all(grad_sums, 'rows', 1, 2, tiled=True).astype(jnp.float32)]
    ppermute x0 -> x3, waiting for transfers between devices: none -> 13.3 us  [sent_to_each(): lax.ppermute(sent, axis, [(i, (i + step) % peers) for i in range(peers)])]
  transfers between devices with their start and end apart: 14 -> 16, of which waited for: 7 -> 9; matrix products, arithmetic and copies ran while one was open for 20% -> 20% of each run, Pallas kernels for 0% -> 0%
where the time goes in v1:
time: 343 us; the launch traced here: 342 us
  waiting for transfers between devices  183 us (53%)
  other arithmetic  42.1 us (12%)
  matrix products  35.8 us (10%)
  starting transfers between devices  34.4 us (10%)
  local copies, waits for them, and re-layouts  31.3 us (9%)
  between operations  15.3 us (4%)
    all_to_all x1, waiting for transfers between devices, body(): up_loc = lax.all_to_all(pieces, ('dp', 'rows'), 0, 0, tiled=True)  44.9 us
    all_gather x1, waiting for transfers between devices, body(): down_loc = lax.all_gather(down_loc, 'dp', axis=1, tiled=True)  43.2 us
    reduce_scatter x1, waiting for transfers between devices, body(): lax.psum_scatter(jnp.stack([mlp_terms, norm_terms]).astype(jnp.bfloat16),...  42.3 us
    reduce_scatter x1, waiting for transfers between devices, body(): lax.psum_scatter(up_part.astype(jnp.bfloat16), 'dp', scatter_dimension=0,...  26.9 us
    ppermute x3, waiting for transfers between devices, sent_to_each(): lax.ppermute(sent, axis, [(i, (i + step) % peers) for i in range(peers)])  13.3 us
    reduce_sum x1, other arithmetic, body(): average = jnp.mean(flat, axis=-1, keepdims=True)  9.44 us
    convert_element_type x1, other arithmetic, body(): grad_x = (d_out.astype(jnp.float32) + back_conv).astype(jnp.bfloat16)  8.33 us
    dot_general x1, matrix products, body(): hidden = jnp.dot(gathered, up_loc, preferred_element_type=jnp.float32)  7.49 us
  transfers between devices with their start and end apart: 16, of which 9 were waited for; matrix products, arithmetic and copies ran while one was open for 20% of the time, Pallas kernels for 0%

profile of v1, /device:TPU:0, one launch (start us, length us, event | category | flops | bytes accessed | tf_op | source)
XLA Modules:
  0.0 342.0 jit_solution(15026360710991722096)
XLA Ops:
  7.2 1.1 fusion.116
  8.3 2.4 collective-permute-start
  10.7 1.3 collective-permute-start.1
  12.0 1.4 slice_reduce_fusion.48
  13.5 1.8 slice_reduce_fusion.50
  15.6 2.4 slice_reduce_fusion.49
  18.1 1.1 maximum_convert_fusion
  19.2 9.4 %fusion.112 = (f32[4,32]{1,0:T(4,128)S(1)}, f32[1,4,32,1536]{3,2,1,0:T(8,128)S(1)}) fusion(f32[1536]{0:T(1024)S(1)} %get-tuple-element.119, f32[1536]{0:T(1024)S(1)} %get-tuple-element.120, f32[1536]{0:T(1024)S(1)} %get-tuple-element.73, f32[1536]{0:T(1024)S(1)} %get-tuple-element.74, f32[1,10,32,1536]{3,2,1,0:T(8,128)S(1)} %maximum_convert_fusion, ...), kind=kLoop, calls=%fused_computation.345 | loop fusion | flops 19267456 | bytes 8641024 | tf_op jit(solution)/shard_map/reduce_sum | solution.py:103
  29.8 0.9 pad_maximum_fusion.3
  31.1 0.9 copy.38
  31.9 6.1 %all-to-all-start.1 = ((bf16[4,768,96]{1,2,0:T(8,128)(2,1)}), bf16[4,768,96]{1,2,0:T(8,128)(2,1)S(1)}, u32[]{:S(2)}, u32[]{:S(2)}) async-start(bf16[4,768,96]{1,2,0:T(8,128)(2,1)} %bitcast.106), calls=%async_computation.1 | async-start | bytes 1179648 | tf_op jit(solution)/shard_map/all_to_all | solution.py:88
  38.1 2.5 reshape.616
  40.5 2.0 copy.28
  42.5 7.0 %all-to-all-done.1 = bf16[4,768,96]{1,2,0:T(8,128)(2,1)S(1)} async-done(((bf16[4,768,96]{1,2,0:T(8,128)(2,1)}), bf16[4,768,96]{1,2,0:T(8,128)(2,1)S(1)}, u32[]{:S(2)}, u32[]{:S(2)}) %all-to-all-start.1) | async-done | bytes 589856 | tf_op jit(solution)/shard_map/all_to_all | solution.py:88
  49.5 2.9 broadcast_in_dim.8
  52.4 5.3 %all-to-all-start = ((bf16[16,96,768]{2,1,0:T(8,128)(2,1)}), bf16[16,96,768]{2,1,0:T(8,128)(2,1)}, u32[]{:S(2)}, u32[]{:S(2)}) async-start(bf16[16,96,768]{2,1,0:T(8,128)(2,1)} %bitcast.98), calls=%async_computation | async-start | bytes 4718592 | tf_op jit(solution)/shard_map/all_to_all | solution.py:86
  57.8 0.7 all-gather.5.cloned.1.call-update
  58.7 44.9 %all-to-all-done = bf16[16,96,768]{2,1,0:T(8,128)(2,1)} async-done(((bf16[16,96,768]{2,1,0:T(8,128)(2,1)}), bf16[16,96,768]{2,1,0:T(8,128)(2,1)}, u32[]{:S(2)}, u32[]{:S(2)}) %all-to-all-start) | async-done | bytes 2359328 | tf_op jit(solution)/shard_map/all_to_all | solution.py:86
  103.6 7.5 %multiply_convert_fusion = (bf16[1024,768]{1,0:T(8,128)(2,1)}, f32[1024,768]{1,0:T(8,128)}) fusion(bf16[1536,768]{1,0:T(8,128)(2,1)} %bitcast.5, bf16[2,1024,1536]{2,1,0:T(8,128)(2,1)} %all-gather.3.cloned.1.call-done), kind=kOutput, calls=%fused_computation.101 | convolution fusion | flops 2419851264 | bytes 10223616 | tf_op jit(solution)/shard_map/dot_general | solution.py:111
  111.1 43.2 %all-gather.5.cloned.1.call-done = bf16[768,1536]{0,1:T(8,128)(2,1)} async-done(((bf16[768,384]{0,1:T(8,128)(2,1)}), bf16[768,1536]{0,1:T(8,128)(2,1)}) %all-gather.5.cloned.1.call-update) | async-done | bytes 2359312 | tf_op jit(solution)/shard_map/all_gather | solution.py:89
  154.3 6.6 %fusion.7 = bf16[1024,768]{1,0:T(8,128)(2,1)S(1)} fusion(f32[1024,768]{1,0:T(8,128)} %get-tuple-element.138, bf16[768,1536]{0,1:T(8,128)(2,1)} %all-gather.5.cloned.1.call-done, bf16[2,1024,1536]{2,1,0:T(8,128)(2,1)} %all-gather.3.cloned.1.call-done), kind=kOutput, calls=%fused_computation.98 | convolution fusion | flops 2423783424 | bytes 10223616 | tf_op jit(solution)/shard_map/dot_general | solution.py:117
  161.0 5.1 %fusion.1 = bf16[1,1024,1536]{2,1,0:T(8,128)(2,1)S(1)} fusion(bf16[1024,768]{1,0:T(8,128)(2,1)S(1)} %fusion.7, bf16[1536,768]{1,0:T(8,128)(2,1)} %bitcast.5), kind=kOutput, calls=%fused_computation.92 | convolution fusion | flops 2417491968 | bytes 7077888 | tf_op jit(solution)/shard_map/dot_general | solution.py:124
  166.2 2.9 fusion
  169.1 3.2 pad_maximum_fusion
  172.6 6.5 %convolution_convert_fusion.3 = bf16[1536,768]{1,0:T(8,128)(2,1)} fusion(bf16[1024,768]{1,0:T(8,128)(2,1)} %copy-done.62, bf16[2,1024,1536]{2,1,0:T(8,128)(2,1)} %all-gather.3.cloned.1.call-done), kind=kOutput, calls=%fused_computation.90 | convolution fusion | flops 2417098752 | bytes 7077888 | tf_op jit(solution)/shard_map/dot_general | solution.py:121
  179.1 7.2 %convolution_convert_fusion.2 = bf16[1536,768]{1,0:T(8,128)(2,1)} fusion(bf16[1024,768]{1,0:T(8,128)(2,1)} %get-tuple-element.137, bf16[2,1024,1536]{2,1,0:T(8,128)(2,1)} %all-gather.3.cloned.1.call-done), kind=kOutput, calls=%fused_computation.89 | convolution fusion | flops 2417098752 | bytes 7077888 | tf_op jit(solution)/shard_map/dot_general | solution.py:114
  186.2 4.5 %all-to-all-start.2 = ((bf16[4,384,768]{2,1,0:T(8,128)(2,1)}), bf16[4,384,768]{2,1,0:T(8,128)(2,1)}, u32[]{:S(2)}, u32[]{:S(2)}) async-start(bf16[4,384,768]{2,1,0:T(8,128)(2,1)} %bitcast.104), calls=%async_computation.4 | async-start | bytes 4718592 | tf_op jit(solution)/shard_map/all_to_all | solution.py:138
  190.7 42.3 %reduce-scatter.3.cloned.1.call-done = bf16[2,128,1536]{2,1,0:T(8,128)(2,1)} async-done(((bf16[2,1024,1536]{2,1,0:T(8,128)(2,1)}), bf16[2,128,1536]{2,1,0:T(8,128)(2,1)}) %reduce-scatter.3.cloned.1.call-update) | async-done | bytes 786448 | tf_op jit(solution)/shard_map/reduce_scatter | solution.py:127
  233.0 1.4 convert_element_type.117
  234.4 2.1 fusion.104
  236.5 0.6 broadcast_in_dim.9
  237.6 1.3 div.22
  238.9 1.2 broadcast_multiply_fusion.1
  240.1 1.3 div.24
  241.4 1.3 broadcast_in_dim.10
  242.7 1.0 fusion.114
  243.7 2.4 multiply_reduce_fusion
  246.4 2.0 multiply_reduce_fusion.18
  248.4 1.4 multiply_reduce_fusion.36
  250.9 1.0 reshape.621
  251.8 4.7 %all-to-all-start.3 = ((f32[32,2,1536]{2,1,0:T(2,128)}), f32[32,2,1536]{2,1,0:T(2,128)}, u32[]{:S(2)}, u32[]{:S(2)}) async-start(f32[32,2,1536]{2,1,0:T(2,128)} %reshape.621), calls=%async_computation.5 | async-start | bytes 786432 | tf_op jit(solution)/shard_map/all_to_all | solution.py:69
  256.6 2.1 collective-permute-start.2
  258.7 1.6 collective-permute-start.3
  260.9 2.3 reduce_sum.518
  263.2 26.9 %reduce-scatter.5.cloned.1.call-done = bf16[384,768]{1,0:T(8,128)(2,1)} async-done(((bf16[1536,768]{1,0:T(8,128)(2,1)}), bf16[384,768]{1,0:T(8,128)(2,1)}) %reduce-scatter.5.cloned.1.call-update) | async-done | bytes 589840 | tf_op jit(solution)/shard_map/reduce_scatter | solution.py:139
  290.1 1.2 pad_maximum_fusion.1
  291.3 0.7 copy-done.6
  292.0 1.2 maximum_convert_fusion.1
  293.3 1.1 reduce_sum.572
  294.4 0.8 broadcast_in_dim.11
  295.2 4.8 %all-to-all-start.4 = ((f32[32,2,1536]{2,1,0:T(2,128)}), f32[32,2,1536]{2,1,0:T(2,128)S(1)}, u32[]{:S(2)}, u32[]{:S(2)}) async-start(f32[32,2,1536]{2,1,0:T(2,128)} %broadcast_in_dim.11), calls=%async_computation.6 | async-start | bytes 786432 | tf_op jit(solution)/shard_map/all_to_all | solution.py:71
  300.0 8.3 %fusion.97 = bf16[1,4,32,1536]{3,2,1,0:T(8,128)(2,1)} fusion(f32[1,10,32,1536]{3,2,1,0:T(8,128)S(1)} %maximum_convert_fusion.1, f32[1536]{0:T(1024)} %copy-done.17, f32[1536]{0:T(1024)} %copy-done.18, f32[1536]{0:T(1024)} %copy-done.20, f32[1536]{0:T(1024)} %copy-done.21, f32[1536]{0:T(1024)} %copy-done.22, f32[1536]{0:T(1024)} %copy-done.23, ...), kind=kLoop, calls=%fused_computation.197 | loop fusion | flops 19660800 | bytes 8562688 | tf_op jit(solution)/shard_map/convert_element_type | solution.py:165
  308.4 4.8 %all-to-all-done.4 = f32[32,2,1536]{2,1,0:T(2,128)S(1)} async-done(((f32[32,2,1536]{2,1,0:T(2,128)}), f32[32,2,1536]{2,1,0:T(2,128)S(1)}, u32[]{:S(2)}, u32[]{:S(2)}) %all-to-all-start.4) | async-done | bytes 393248 | tf_op jit(solution)/shard_map/all_to_all | solution.py:71
  313.5 0.6 slice_reduce_fusion
  314.1 0.8 reshape.623
  315.0 0.6 collective-permute-start.6
  316.1 0.8 add_convert_fusion
  316.9 6.0 %collective-permute-done.6 = bf16[2,96,768]{2,1,0:T(8,128)(2,1)S(1)} collective-permute-done((bf16[2,96,768]{2,1,0:T(8,128)(2,1)S(1)}, bf16[2,96,768]{2,1,0:T(8,128)(2,1)S(1)}, u32[]{:S(2)}, u32[]{:S(2)}) %collective-permute-start.6) | collective-permute-done | bytes 294944 | tf_op jit(solution)/shard_map/ppermute | solution.py:33
  322.9 6.8 %collective-permute-done.5 = bf16[2,96,768]{2,1,0:T(8,128)(2,1)S(1)} collective-permute-done((bf16[2,96,768]{2,1,0:T(8,128)(2,1)S(1)}, bf16[2,96,768]{2,1,0:T(8,128)(2,1)S(1)}, u32[]{:S(2)}, u32[]{:S(2)}) %collective-permute-start.5) | collective-permute-done | bytes 294944 | tf_op jit(solution)/shard_map/ppermute | solution.py:33
  330.4 0.7 gather_fusion
  331.5 0.8 copy.32
  332.3 1.2 copy.36
  333.5 0.8 copy.31
  334.3 1.2 copy.35
  (209 shorter events, 5.7 us)
Async XLA Ops:
  7.2 96.4 %all-gather.3.cloned.1.call-start = ((), (), s32[]{:S(2)}) async-start(), calls=%async_computation.7 | async-start | bytes 7077888 | tf_op jit(solution)/shard_map/all_gather | solution.py:109
  8.3 9.7 %collective-permute-start = (bf16[1,3,32,1536]{3,2,1,0:T(8,128)(2,1)S(1)}, bf16[1,3,32,1536]{3,2,1,0:T(8,128)(2,1)S(1)}, u32[]{:S(2)}, u32[]{:S(2)}) collective-permute-start(bf16[1,3,32,1536]{3,2,1,0:T(8,128)(2,1)S(1)} %get-tuple-element.135), channel_id=1, source_target_pairs={{0,1},{1,2},{2,3},{4,5},{5,6},{6,7},{8,9},{9,10},{10,11},{12,13},{... | collective-permute-start | bytes 884744 | tf_op jit(solution)/shard_map/ppermute | solution.py:45
  10.7 7.3 %collective-permute-start.1 = (bf16[1,3,32,1536]{3,2,1,0:T(8,128)(2,1)S(1)}, bf16[1,3,32,1536]{3,2,1,0:T(8,128)(2,1)S(1)}, u32[]{:S(2)}, u32[]{:S(2)}) collective-permute-start(bf16[1,3,32,1536]{3,2,1,0:T(8,128)(2,1)S(1)} %get-tuple-element.136), channel_id=1, source_target_pairs={{1,0},{2,1},{3,2},{5,4},{6,5},{7,6},{9,8},{10,9},{11,10},{13,12},{... | collective-permute-start | bytes 884744 | tf_op jit(solution)/shard_map/ppermute | solution.py:46
  13.4 15.3 %copy-start.8 = (f32[1536]{0:T(1024)}, f32[1536]{0:T(1024)S(1)}, u32[]{:S(2)}) copy-start(f32[1536]{0:T(1024)S(1)} %get-tuple-element.111) | copy-start | bytes 18436
  13.4 15.3 %copy-start.10 = (f32[1536]{0:T(1024)}, f32[1536]{0:T(1024)S(1)}, u32[]{:S(2)}) copy-start(f32[1536]{0:T(1024)S(1)} %get-tuple-element.112) | copy-start | bytes 18436
  13.4 15.3 %copy-start.11 = (f32[1536]{0:T(1024)}, f32[1536]{0:T(1024)S(1)}, u32[]{:S(2)}) copy-start(f32[1536]{0:T(1024)S(1)} %get-tuple-element.113) | copy-start | bytes 18436
  13.4 15.3 %copy-start.12 = (f32[1536]{0:T(1024)}, f32[1536]{0:T(1024)S(1)}, u32[]{:S(2)}) copy-start(f32[1536]{0:T(1024)S(1)} %get-tuple-element.114) | copy-start | bytes 18436
  13.5 15.3 %copy-start.13 = (f32[1536]{0:T(1024)}, f32[1536]{0:T(1024)S(1)}, u32[]{:S(2)}) copy-start(f32[1536]{0:T(1024)S(1)} %get-tuple-element.115) | copy-start | bytes 18436
  13.5 15.3 %copy-start.14 = (f32[1536]{0:T(1024)}, f32[1536]{0:T(1024)S(1)}, u32[]{:S(2)}) copy-start(f32[1536]{0:T(1024)S(1)} %get-tuple-element.116) | copy-start | bytes 18436
  13.5 15.3 %copy-start.15 = (f32[1536]{0:T(1024)}, f32[1536]{0:T(1024)S(1)}, u32[]{:S(2)}) copy-start(f32[1536]{0:T(1024)S(1)} %get-tuple-element.117) | copy-start | bytes 18436
  13.5 15.3 %copy-start.16 = (f32[1536]{0:T(1024)}, f32[1536]{0:T(1024)S(1)}, u32[]{:S(2)}) copy-start(f32[1536]{0:T(1024)S(1)} %get-tuple-element.118) | copy-start | bytes 18436
  13.5 15.3 %copy-start.17 = (f32[1536]{0:T(1024)}, f32[1536]{0:T(1024)S(1)}, u32[]{:S(2)}) copy-start(f32[1536]{0:T(1024)S(1)} %get-tuple-element.119) | copy-start | bytes 18436
  13.5 15.3 %copy-start.18 = (f32[1536]{0:T(1024)}, f32[1536]{0:T(1024)S(1)}, u32[]{:S(2)}) copy-start(f32[1536]{0:T(1024)S(1)} %get-tuple-element.120) | copy-start | bytes 18436
  15.4 13.4 %copy-start.19 = (f32[1536]{0:T(1024)}, f32[1536]{0:T(1024)S(1)}, u32[]{:S(2)}) copy-start(f32[1536]{0:T(1024)S(1)} %get-tuple-element.72) | copy-start | bytes 18436
  15.4 13.4 %copy-start.20 = (f32[1536]{0:T(1024)}, f32[1536]{0:T(1024)S(1)}, u32[]{:S(2)}) copy-start(f32[1536]{0:T(1024)S(1)} %get-tuple-element.73) | copy-start | bytes 18436
  15.4 13.4 %copy-start.21 = (f32[1536]{0:T(1024)}, f32[1536]{0:T(1024)S(1)}, u32[]{:S(2)}) copy-start(f32[1536]{0:T(1024)S(1)} %get-tuple-element.74) | copy-start | bytes 18436
  15.4 13.4 %copy-start.22 = (f32[1536]{0:T(1024)}, f32[1536]{0:T(1024)S(1)}, u32[]{:S(2)}) copy-start(f32[1536]{0:T(1024)S(1)} %get-tuple-element.75) | copy-start | bytes 18436
  15.4 13.4 %copy-start.23 = (f32[1536]{0:T(1024)}, f32[1536]{0:T(1024)S(1)}, u32[]{:S(2)}) copy-start(f32[1536]{0:T(1024)S(1)} %get-tuple-element.76) | copy-start | bytes 18436
  15.4 13.4 %copy-start.24 = (f32[1536]{0:T(1024)}, f32[1536]{0:T(1024)S(1)}, u32[]{:S(2)}) copy-start(f32[1536]{0:T(1024)S(1)} %get-tuple-element.77) | copy-start | bytes 18436
  15.4 13.4 %copy-start.25 = (f32[1536]{0:T(1024)}, f32[1536]{0:T(1024)S(1)}, u32[]{:S(2)}) copy-start(f32[1536]{0:T(1024)S(1)} %get-tuple-element.78) | copy-start | bytes 18436
  15.4 13.4 %copy-start.26 = (f32[1536]{0:T(1024)}, f32[1536]{0:T(1024)S(1)}, u32[]{:S(2)}) copy-start(f32[1536]{0:T(1024)S(1)} %get-tuple-element.79) | copy-start | bytes 18436
  15.4 13.4 %copy-start.27 = (f32[1536]{0:T(1024)}, f32[1536]{0:T(1024)S(1)}, u32[]{:S(2)}) copy-start(f32[1536]{0:T(1024)S(1)} %get-tuple-element.80) | copy-start | bytes 18436
  15.5 13.4 %copy-start.28 = (f32[1536]{0:T(1024)}, f32[1536]{0:T(1024)S(1)}, u32[]{:S(2)}) copy-start(f32[1536]{0:T(1024)S(1)} %get-tuple-element.81) | copy-start | bytes 18436
  15.5 13.4 %copy-start.29 = (f32[1536]{0:T(1024)}, f32[1536]{0:T(1024)S(1)}, u32[]{:S(2)}) copy-start(f32[1536]{0:T(1024)S(1)} %get-tuple-element.82) | copy-start | bytes 18436
  15.5 13.4 %copy-start.30 = (f32[1536]{0:T(1024)}, f32[1536]{0:T(1024)S(1)}, u32[]{:S(2)}) copy-start(f32[1536]{0:T(1024)S(1)} %get-tuple-element.83) | copy-start | bytes 18436
  15.5 13.4 %copy-start.31 = (f32[1536]{0:T(1024)}, f32[1536]{0:T(1024)S(1)}, u32[]{:S(2)}) copy-start(f32[1536]{0:T(1024)S(1)} %get-tuple-element.84) | copy-start | bytes 18436
  15.5 13.4 %copy-start.32 = (f32[1536]{0:T(1024)}, f32[1536]{0:T(1024)S(1)}, u32[]{:S(2)}) copy-start(f32[1536]{0:T(1024)S(1)} %get-tuple-element.85) | copy-start | bytes 18436
  15.5 13.4 %copy-start.33 = (f32[1536]{0:T(1024)}, f32[1536]{0:T(1024)S(1)}, u32[]{:S(2)}) copy-start(f32[1536]{0:T(1024)S(1)} %get-tuple-element.86) | copy-start | bytes 18436
  15.5 13.4 %copy-start.34 = (f32[1536]{0:T(1024)}, f32[1536]{0:T(1024)S(1)}, u32[]{:S(2)}) copy-start(f32[1536]{0:T(1024)S(1)} %get-tuple-element.87) | copy-start | bytes 18436
  15.5 13.4 %copy-start.35 = (f32[1536]{0:T(1024)}, f32[1536]{0:T(1024)S(1)}, u32[]{:S(2)}) copy-start(f32[1536]{0:T(1024)S(1)} %get-tuple-element.88) | copy-start | bytes 18436
  15.5 13.4 %copy-start.36 = (f32[1536]{0:T(1024)}, f32[1536]{0:T(1024)S(1)}, u32[]{:S(2)}) copy-start(f32[1536]{0:T(1024)S(1)} %get-tuple-element.89) | copy-start | bytes 18436
  15.5 13.4 %copy-start.37 = (f32[1536]{0:T(1024)}, f32[1536]{0:T(1024)S(1)}, u32[]{:S(2)}) copy-start(f32[1536]{0:T(1024)S(1)} %get-tuple-element.90) | copy-start | bytes 18436
  18.0 11.0 %copy-start.38 = (f32[1536]{0:T(1024)}, f32[1536]{0:T(1024)S(1)}, u32[]{:S(2)}) copy-start(f32[1536]{0:T(1024)S(1)} %get-tuple-element.91) | copy-start | bytes 18436
  18.0 11.0 %copy-start.39 = (f32[1536]{0:T(1024)}, f32[1536]{0:T(1024)S(1)}, u32[]{:S(2)}) copy-start(f32[1536]{0:T(1024)S(1)} %get-tuple-element.92) | copy-start | bytes 18436
  18.0 11.0 %copy-start.40 = (f32[1536]{0:T(1024)}, f32[1536]{0:T(1024)S(1)}, u32[]{:S(2)}) copy-start(f32[1536]{0:T(1024)S(1)} %get-tuple-element.93) | copy-start | bytes 18436
  18.0 11.0 %copy-start.41 = (f32[1536]{0:T(1024)}, f32[1536]{0:T(1024)S(1)}, u32[]{:S(2)}) copy-start(f32[1536]{0:T(1024)S(1)} %get-tuple-element.94) | copy-start | bytes 18436
  18.0 11.0 %copy-start.42 = (f32[1536]{0:T(1024)}, f32[1536]{0:T(1024)S(1)}, u32[]{:S(2)}) copy-start(f32[1536]{0:T(1024)S(1)} %get-tuple-element.95) | copy-start | bytes 18436
  18.0 11.0 %copy-start.43 = (f32[1536]{0:T(1024)}, f32[1536]{0:T(1024)S(1)}, u32[]{:S(2)}) copy-start(f32[1536]{0:T(1024)S(1)} %get-tuple-element.96) | copy-start | bytes 18436
  18.0 11.0 %copy-start.44 = (f32[1536]{0:T(1024)}, f32[1536]{0:T(1024)S(1)}, u32[]{:S(2)}) copy-start(f32[1536]{0:T(1024)S(1)} %get-tuple-element.97) | copy-start | bytes 18436
  18.0 11.0 %copy-start.45 = (f32[1536]{0:T(1024)}, f32[1536]{0:T(1024)S(1)}, u32[]{:S(2)}) copy-start(f32[1536]{0:T(1024)S(1)} %get-tuple-element.98) | copy-start | bytes 18436
  18.0 11.0 %copy-start.46 = (f32[1536]{0:T(1024)}, f32[1536]{0:T(1024)S(1)}, u32[]{:S(2)}) copy-start(f32[1536]{0:T(1024)S(1)} %get-tuple-element.99) | copy-start | bytes 18436
  18.0 11.0 %copy-start.47 = (f32[1536]{0:T(1024)}, f32[1536]{0:T(1024)S(1)}, u32[]{:S(2)}) copy-start(f32[1536]{0:T(1024)S(1)} %get-tuple-element.100) | copy-start | bytes 18436
  19.2 10.3 %copy-start.2 = (bf16[1,4,32,1536]{3,2,1,0:T(8,128)(2,1)S(1)}, bf16[1,4,32,1536]{3,2,1,0:T(8,128)(2,1)}, u32[]{:S(2)}) copy-start(bf16[1,4,32,1536]{3,2,1,0:T(8,128)(2,1)} %param.13) | copy-start | bytes 1179652
  19.2 10.3 %copy-start.7 = (f32[1536]{0:T(1024)S(1)}, f32[1536]{0:T(1024)}, u32[]{:S(2)}) copy-start(f32[1536]{0:T(1024)} %param.9) | copy-start | bytes 18436
  19.2 10.3 %copy-start.48 = (f32[1536]{0:T(1024)S(1)}, f32[1536]{0:T(1024)}, u32[]{:S(2)}) copy-start(f32[1536]{0:T(1024)} %param.12) | copy-start | bytes 18436
  31.9 17.6 %all-to-all-start.1 = ((bf16[4,768,96]{1,2,0:T(8,128)(2,1)}), bf16[4,768,96]{1,2,0:T(8,128)(2,1)S(1)}, u32[]{:S(2)}, u32[]{:S(2)}) async-start(bf16[4,768,96]{1,2,0:T(8,128)(2,1)} %bitcast.106), calls=%async_computation.1 | async-start | bytes 1179648 | tf_op jit(solution)/shard_map/all_to_all | solution.py:88
  52.4 51.2 %all-to-all-start = ((bf16[16,96,768]{2,1,0:T(8,128)(2,1)}), bf16[16,96,768]{2,1,0:T(8,128)(2,1)}, u32[]{:S(2)}, u32[]{:S(2)}) async-start(bf16[16,96,768]{2,1,0:T(8,128)(2,1)} %bitcast.98), calls=%async_computation | async-start | bytes 4718592 | tf_op jit(solution)/shard_map/all_to_all | solution.py:86
  57.7 96.6 %all-gather.5.cloned.1.call-start = ((), (), s32[]{:S(2)}) async-start(), calls=%async_computation.8 | async-start | bytes 2949120 | tf_op jit(solution)/shard_map/all_gather | solution.py:89
  58.5 174.5 %reduce-scatter.3.cloned.1.call-start = ((), (), s32[]{:S(2)}) async-start(), calls=%async_computation.9 | async-start | bytes 7077888 | tf_op jit(solution)/shard_map/reduce_scatter | solution.py:127
  161.0 5.2 %copy-start.62 = (bf16[1024,768]{1,0:T(8,128)(2,1)}, bf16[1024,768]{1,0:T(8,128)(2,1)S(1)}, u32[]{:S(2)}) copy-start(bf16[1024,768]{1,0:T(8,128)(2,1)S(1)} %fusion.7) | copy-start | bytes 4718596
  172.3 117.8 %reduce-scatter.5.cloned.1.call-start = ((), (), s32[]{:S(2)}) async-start(), calls=%async_computation.10 | async-start | bytes 2949120 | tf_op jit(solution)/shard_map/reduce_scatter | solution.py:139
  186.2 65.6 %all-to-all-start.2 = ((bf16[4,384,768]{2,1,0:T(8,128)(2,1)}), bf16[4,384,768]{2,1,0:T(8,128)(2,1)}, u32[]{:S(2)}, u32[]{:S(2)}) async-start(bf16[4,384,768]{2,1,0:T(8,128)(2,1)} %bitcast.104), calls=%async_computation.4 | async-start | bytes 4718592 | tf_op jit(solution)/shard_map/all_to_all | solution.py:138
  233.0 9.7 %copy-start = (bf16[2,128,1536]{2,1,0:T(8,128)(2,1)S(1)}, bf16[2,128,1536]{2,1,0:T(8,128)(2,1)}, u32[]{:S(2)}) copy-start(bf16[2,128,1536]{2,1,0:T(8,128)(2,1)} %reduce-scatter.3.cloned.1.call-done) | copy-start | bytes 2359300
  251.8 41.4 %all-to-all-start.3 = ((f32[32,2,1536]{2,1,0:T(2,128)}), f32[32,2,1536]{2,1,0:T(2,128)}, u32[]{:S(2)}, u32[]{:S(2)}) async-start(f32[32,2,1536]{2,1,0:T(2,128)} %reshape.621), calls=%async_computation.5 | async-start | bytes 786432 | tf_op jit(solution)/shard_map/all_to_all | solution.py:69
  256.6 34.7 %collective-permute-start.2 = (bf16[1,3,32,1536]{3,2,1,0:T(8,128)(2,1)S(1)}, bf16[1,3,32,1536]{3,2,1,0:T(8,128)(2,1)S(1)}, u32[]{:S(2)}, u32[]{:S(2)}) collective-permute-start(bf16[1,3,32,1536]{3,2,1,0:T(8,128)(2,1)S(1)} %get-tuple-element.133), channel_id=1, source_target_pairs={{0,1},{1,2},{2,3},{4,5},{5,6},{6,7},{8,9},{9,10},{10,11},{12,13},{... | collective-permute-start | bytes 884744 | tf_op jit(solution)/shard_map/ppermute | solution.py:45
  258.7 33.3 %collective-permute-start.3 = (bf16[1,3,32,1536]{3,2,1,0:T(8,128)(2,1)S(1)}, bf16[1,3,32,1536]{3,2,1,0:T(8,128)(2,1)}, u32[]{:S(2)}, u32[]{:S(2)}) collective-permute-start(bf16[1,3,32,1536]{3,2,1,0:T(8,128)(2,1)S(1)} %get-tuple-element.134), channel_id=1, source_target_pairs={{1,0},{2,1},{3,2},{5,4},{6,5},{7,6},{9,8},{10,9},{11,10},{13,12},{... | collective-permute-start | bytes 884744 | tf_op jit(solution)/shard_map/ppermute | solution.py:46
  291.3 8.7 %copy-start.9 = (f32[1536]{0:T(1024)S(1)}, f32[1536]{0:T(1024)}, u32[]{:S(2)}) copy-start(f32[1536]{0:T(1024)} %copy-done.8) | copy-start | bytes 18436
  295.2 18.0 %all-to-all-start.4 = ((f32[32,2,1536]{2,1,0:T(2,128)}), f32[32,2,1536]{2,1,0:T(2,128)S(1)}, u32[]{:S(2)}, u32[]{:S(2)}) async-start(f32[32,2,1536]{2,1,0:T(2,128)} %broadcast_in_dim.11), calls=%async_computation.6 | async-start | bytes 786432 | tf_op jit(solution)/shard_map/all_to_all | solution.py:71
  308.4 7.7 %copy-start.1 = (bf16[1,4,32,1536]{3,2,1,0:T(8,128)(2,1)S(1)}, bf16[1,4,32,1536]{3,2,1,0:T(8,128)(2,1)}, u32[]{:S(2)}) copy-start(bf16[1,4,32,1536]{3,2,1,0:T(8,128)(2,1)} %param.7) | copy-start | bytes 1179652
  308.4 7.7 %copy-start.3 = (f32[1,128,1536]{2,1,0:T(8,128)S(1)}, f32[1,128,1536]{2,1,0:T(8,128)}, u32[]{:S(2)}) copy-start(f32[1,128,1536]{2,1,0:T(8,128)} %get-tuple-element.132) | copy-start | bytes 2359300
  308.4 7.7 %copy-start.49 = (f32[1536]{0:T(1024)S(1)}, f32[1536]{0:T(1024)}, u32[]{:S(2)}) copy-start(f32[1536]{0:T(1024)} %param.12) | copy-start | bytes 18436
  315.0 8.0 %collective-permute-start.6 = (bf16[2,96,768]{2,1,0:T(8,128)(2,1)S(1)}, bf16[2,96,768]{2,1,0:T(8,128)(2,1)S(1)}, u32[]{:S(2)}, u32[]{:S(2)}) collective-permute-start(bf16[2,96,768]{2,1,0:T(8,128)(2,1)S(1)} %get-tuple-element.127), channel_id=1, source_target_pairs={{0,3},{1,0},{2,1},{3,2},{4,7},{5,4},{6,5},{7,6},{8,11},{9,8},{10,9... | collective-permute-start | bytes 884744 | tf_op jit(solution)/shard_map/ppermute | solution.py:33
  315.6 14.2 %collective-permute-start.5 = (bf16[2,96,768]{2,1,0:T(8,128)(2,1)S(1)}, bf16[2,96,768]{2,1,0:T(8,128)(2,1)S(1)}, u32[]{:S(2)}, u32[]{:S(2)}) collective-permute-start(bf16[2,96,768]{2,1,0:T(8,128)(2,1)S(1)} %get-tuple-element.128), channel_id=1, source_target_pairs={{0,2},{1,3},{2,0},{3,1},{4,6},{5,7},{6,4},{7,5},{8,10},{9,11},{10,... | collective-permute-start | bytes 884744 | tf_op jit(solution)/shard_map/ppermute | solution.py:33
  316.1 14.2 %collective-permute-start.4 = (bf16[2,96,768]{2,1,0:T(8,128)(2,1)S(1)}, bf16[2,96,768]{2,1,0:T(8,128)(2,1)S(1)}, u32[]{:S(2)}, u32[]{:S(2)}) collective-permute-start(bf16[2,96,768]{2,1,0:T(8,128)(2,1)S(1)} %get-tuple-element.129), channel_id=1, source_target_pairs={{0,1},{1,2},{2,3},{3,0},{4,5},{5,6},{6,7},{7,4},{8,9},{9,10},{10,1... | collective-permute-start | bytes 884744 | tf_op jit(solution)/shard_map/ppermute | solution.py:33
  (15 other events, 36.5 us)
Sparse Core Ops, SparseCore 0:
  30.9 67.5 all-gather.2
  100.7 53.6 all-gather.4
  172.4 60.5 reduce-scatter.2
  235.3 54.7 reduce-scatter.4
